TPU v7x, 256 devices: a whole 4x4x8 slice. The times are simulated.
256 devices in a mesh: grp: 4 (over y_hi, core), tile: 64 (over y_lo, x, z).
Axes of the slice: x: 4, y: 4 (y_hi: 2, y_lo: 2; y = y_hi * 2 + y_lo), z: 8, core: 2. Of those that a mesh axis runs over, the one named last changes fastest.
Arguments:
- frames: float32 [4, 2048, 2048], P('grp', 'tile'), may hold values from -6 to 6
- otf: float32 [4, 2, 2048, 2048], P('grp', None, 'tile'), may hold values from -6 to 6, as said below
- start_image: float32 [2048, 2048], P('tile'), may hold values from -6 to 6
Outputs:
- consensus: float32 [2048, 2048], P('tile')
Inputs may be any that keep to these rules, and one draw needn't show every extreme that they name: Transfer functions of real point spread functions: otf[f, 0, t, s] equals otf[f, 0, -t, -s] and otf[f, 1, t, s] equals -otf[f, 1, -t, -s], indices taken modulo 2048.
All inputs are finite; a program needn't handle non-finite values.
Results may differ from a plain program's by a relative error of at most 0.0001.
Values sent between devices are 32-bit elements; how exact they have to be, the bound alone decides.
No kernel may reach another device: no remote copies, remote signals or barrier semaphores. Data moves between devices by JAX's collectives and lax.ppermute only.
A program may use at most 64 MiB of HBM per device.

v0:
```python
import math
import jax
import jax.numpy as jnp
from jax import lax
from jax.sharding import PartitionSpec as P

ITERS = 2
TV_ITERS = 4
penalty = 1.0
smooth_weight = 0.25
dual_step = 0.125
highest = lax.Precision.HIGHEST


def from_behind(value, axis, steps):
    count = lax.axis_size(axis)
    leading, last = (max(0, -steps), min(count, count - steps))
    return lax.ppermute(value, axis, [(source, source + steps) for source in range(leading, last)])


def angle_table(first_count, second_count, modulus):
    left_index = jnp.arange(first_count, dtype=jnp.int32)[:, None]
    right_index = jnp.arange(second_count, dtype=jnp.int32)[None, :]
    return (left_index * right_index % modulus).astype(jnp.float32) * (2.0 * math.pi / modulus)


def transform_last(real_part, imag_part, sign_value):
    extent = real_part.shape[-1]
    inner_size = 16
    outer_size = extent // inner_size
    leading = real_part.shape[:-1]
    first_angle = angle_table(inner_size, inner_size, inner_size)
    first_cos = jnp.cos(first_angle)
    first_sin = sign_value * jnp.sin(first_angle)
    split_real = real_part.reshape(leading + (inner_size, outer_size))
    mixed_real = jnp.einsum("...an,ak->...kn", split_real, first_cos, precision=highest)
    mixed_imag = jnp.einsum("...an,ak->...kn", split_real, first_sin, precision=highest)
    if imag_part is not None:
        split_imag = imag_part.reshape(leading + (inner_size, outer_size))
        mixed_real = mixed_real - jnp.einsum(
            "...an,ak->...kn", split_imag, first_sin, precision=highest
        )
        mixed_imag = mixed_imag + jnp.einsum(
            "...an,ak->...kn", split_imag, first_cos, precision=highest
        )
    twist_angle = angle_table(inner_size, outer_size, extent)
    twist_cos = jnp.cos(twist_angle)
    twist_sin = sign_value * jnp.sin(twist_angle)
    turned_real = mixed_real * twist_cos - mixed_imag * twist_sin
    turned_imag = mixed_real * twist_sin + mixed_imag * twist_cos
    second_angle = angle_table(outer_size, outer_size, outer_size)
    second_cos = jnp.cos(second_angle)
    second_sin = sign_value * jnp.sin(second_angle)
    out_real = jnp.einsum(
        "...kn,nj->...jk", turned_real, second_cos, precision=highest
    ) - jnp.einsum("...kn,nj->...jk", turned_imag, second_sin, precision=highest)
    out_imag = jnp.einsum(
        "...kn,nj->...jk", turned_real, second_sin, precision=highest
    ) + jnp.einsum("...kn,nj->...jk", turned_imag, second_cos, precision=highest)
    return (out_real.reshape(leading + (extent,)), out_imag.reshape(leading + (extent,)))


def regroup(moved, frame_count, tile_rows, extent):
    tiles = extent // tile_rows
    moved = moved.reshape(tile_rows, tiles, 2, frame_count, tile_rows)
    return jnp.transpose(moved, (2, 3, 0, 1, 4)).reshape(2, frame_count, tile_rows, extent)


def to_spectrum(images):
    frame_count, tile_rows, extent = images.shape
    col_real, col_imag = transform_last(images, None, -1.0)
    packed = jnp.transpose(jnp.stack([col_real, col_imag]), (3, 0, 1, 2)).reshape(
        extent, 2 * frame_count * tile_rows
    )
    moved = lax.all_to_all(packed, "tile", split_axis=0, concat_axis=1, tiled=True)
    moved = regroup(moved, frame_count, tile_rows, extent)
    return transform_last(moved[0], moved[1], -1.0)


def to_image(spec_real, spec_imag):
    frame_count, tile_rows, extent = spec_real.shape
    row_real, row_imag = transform_last(spec_real, spec_imag, 1.0)
    packed = jnp.transpose(jnp.stack([row_real, row_imag]), (3, 0, 1, 2)).reshape(
        extent, 2 * frame_count * tile_rows
    )
    moved = lax.all_to_all(packed, "tile", split_axis=0, concat_axis=1, tiled=True)
    moved = regroup(moved, frame_count, tile_rows, extent)
    image_parts = transform_last(moved[0], moved[1], 1.0)
    return image_parts[0] / float(extent * extent)


def denoise_sweeps(average):
    tile_rows, extent = average.shape
    on_last = lax.axis_index("tile") == lax.axis_size("tile") - 1
    row_index = jnp.arange(tile_rows, dtype=jnp.int32)[:, None]
    col_index = jnp.arange(extent, dtype=jnp.int32)[None, :]
    keep_rows = jnp.where((row_index == tile_rows - 1) & on_last, 0.0, 1.0).astype(jnp.float32)
    keep_cols = jnp.where(col_index == extent - 1, 0.0, 1.0).astype(jnp.float32)
    zero_col = jnp.zeros((tile_rows, 1), jnp.float32)

    def divergence(downward, sideways):
        above = from_behind(downward[-1:], "tile", 1)
        prev_rows = jnp.concatenate([above, downward[:-1]], 0)
        prev_cols = jnp.concatenate([zero_col, sideways[:, :-1]], 1)
        return downward - prev_rows + sideways - prev_cols

    downward = jnp.zeros_like(average)
    sideways = jnp.zeros_like(average)
    for sweep_index in range(TV_ITERS):
        target = divergence(downward, sideways) - average / smooth_weight
        below = from_behind(target[:1], "tile", -1)
        next_rows = jnp.concatenate([target[1:], below], 0)
        grad_down = (next_rows - target) * keep_rows
        grad_side = (jnp.concatenate([target[:, 1:], zero_col], 1) - target) * keep_cols
        grad_down, grad_side = (grad_down, grad_side)
        scaling = 1.0 + dual_step * jnp.sqrt(grad_down * grad_down + grad_side * grad_side)
        downward = (downward + dual_step * grad_down) / scaling
        sideways = (sideways + dual_step * grad_side) / scaling
    return average - smooth_weight * divergence(downward, sideways)


def denoise(average):
    return denoise_sweeps(average)


def body(frames, otf, start_image):
    frame_count = frames.shape[0]
    total_frames = float(frame_count * lax.axis_size("grp"))
    response_real = otf[:, 0]
    response_imag = otf[:, 1]
    gain = 1.0 / (response_real * response_real + response_imag * response_imag + penalty)
    data_real, data_imag = to_spectrum(frames)
    weighted_real = response_real * data_real + response_imag * data_imag
    weighted_imag = response_real * data_imag - response_imag * data_real
    consensus = start_image
    duals = jnp.zeros_like(frames)
    for iteration in range(ITERS):
        shifted_real, shifted_imag = to_spectrum(consensus[None] - duals)
        estimates = to_image(
            (weighted_real + penalty * shifted_real) * gain,
            (weighted_imag + penalty * shifted_imag) * gain,
        )
        partial_sum = jnp.sum(estimates + duals, axis=0)
        average = lax.psum(partial_sum, "grp") / total_frames
        consensus = denoise(average)
        duals = duals + estimates - consensus[None]
    return consensus


def solution(mesh):
    placed = (P("grp", "tile", None), P("grp", None, "tile", None), P("tile", None))
    return jax.shard_map(
        body, mesh=mesh, in_specs=placed, out_specs=P("tile", None), check_vma=False
    )
```

profile of v0, /device:TPU:8, one launch (start us, length us, event | category | flops | bytes accessed | tf_op | source)
XLA Modules:
  0.0 440.0 jit_solution(548711309243718294)
XLA Ops:
  15.9 13.3 %all-to-all-start.1 = ((f32[64,1,2048]{2,1,0:T(1,128)}), f32[64,1,2048]{2,1,0:T(1,128)S(1)}, u32[]{:S(2)}, u32[]{:S(2)}) async-start(f32[64,1,2048]{2,1,0:T(1,128)} %reshape.646), calls=%async_computation.1 | async-start | bytes 1048576 | tf_op jit(solution)/shard_map/all_to_all | solution.py:75
  30.2 17.7 %all-to-all-done.1 = f32[64,1,2048]{2,1,0:T(1,128)S(1)} async-done(((f32[64,1,2048]{2,1,0:T(1,128)}), f32[64,1,2048]{2,1,0:T(1,128)S(1)}, u32[]{:S(2)}, u32[]{:S(2)}) %all-to-all-start.1) | async-done | bytes 524320 | tf_op jit(solution)/shard_map/all_to_all | solution.py:75
  62.8 5.0 %all-to-all-start = ((f32[64,1,2048]{2,1,0:T(1,128)}), f32[64,1,2048]{2,1,0:T(1,128)S(1)}, u32[]{:S(2)}, u32[]{:S(2)}) async-start(f32[64,1,2048]{2,1,0:T(1,128)} %reshape.644), calls=%async_computation | async-start | bytes 1048576 | tf_op jit(solution)/shard_map/all_to_all | solution.py:75
  73.8 12.0 %all-to-all-done = f32[64,1,2048]{2,1,0:T(1,128)S(1)} async-done(((f32[64,1,2048]{2,1,0:T(1,128)}), f32[64,1,2048]{2,1,0:T(1,128)S(1)}, u32[]{:S(2)}, u32[]{:S(2)}) %all-to-all-start) | async-done | bytes 524320 | tf_op jit(solution)/shard_map/all_to_all | solution.py:75
  107.3 22.4 %all_to_all.80 = f32[64,1,2048]{2,1,0:T(1,128)S(1)} all-to-all(f32[64,1,2048]{2,1,0:T(1,128)S(1)} %reshape.648), channel_id=1, replica_groups=mesh['grp'=4,'tile'=64] {'tile'}, dimensions={0} | all-to-all | bytes 1048576 | tf_op jit(solution)/shard_map/all_to_all | solution.py:86
  141.4 6.9 %collective-permute-done = f32[1,2048]{1,0:T(1,128)S(1)} collective-permute-done((f32[1,2048]{1,0:T(1,128)S(1)}, f32[1,2048]{1,0:T(1,128)S(1)}, u32[]{:S(2)}, u32[]{:S(2)}) %collective-permute-start) | collective-permute-done | bytes 8224 | tf_op jit(solution)/shard_map/ppermute | solution.py:18
  148.4 30.6 %all-reduce.20.cloned.1.call-done = f32[32,2048]{1,0:T(8,128)} async-done(((f32[32,2048]{1,0:T(8,128)}), f32[32,2048]{1,0:T(8,128)}) %all-reduce.20.cloned.1.call-update) | async-done | bytes 262160 | tf_op jit(solution)/shard_map/psum | solution.py:144
  180.1 8.2 %collective-permute-start.1 = (f32[1,2048]{1,0:T(1,128)S(1)}, f32[1,2048]{1,0:T(1,128)S(1)}, u32[]{:S(2)}, u32[]{:S(2)}) collective-permute-start(f32[1,2048]{1,0:T(1,128)S(1)} %slice.257), channel_id=1, source_target_pairs={{1,0},{2,1},{3,2},{4,3},{5,4},{6,5},{7,6},{8,7},{9,8},{10,9},{11,1... | collective-permute-start | bytes 24584 | tf_op jit(solution)/shard_map/ppermute | solution.py:18
  192.8 8.1 %collective-permute-done.2 = f32[1,2048]{1,0:T(1,128)S(1)} collective-permute-done((f32[1,2048]{1,0:T(1,128)S(1)}, f32[1,2048]{1,0:T(1,128)S(1)}, u32[]{:S(2)}, u32[]{:S(2)}) %collective-permute-start.2) | collective-permute-done | bytes 8224 | tf_op jit(solution)/shard_map/ppermute | solution.py:18
  201.0 3.9 collective-permute-start.3
  208.8 7.8 %collective-permute-done.4 = f32[1,2048]{1,0:T(1,128)S(1)} collective-permute-done((f32[1,2048]{1,0:T(1,128)S(1)}, f32[1,2048]{1,0:T(1,128)S(1)}, u32[]{:S(2)}, u32[]{:S(2)}) %collective-permute-start.4) | collective-permute-done | bytes 8224 | tf_op jit(solution)/shard_map/ppermute | solution.py:18
  216.8 3.9 collective-permute-start.5
  224.6 7.8 %collective-permute-done.6 = f32[1,2048]{1,0:T(1,128)S(1)} collective-permute-done((f32[1,2048]{1,0:T(1,128)S(1)}, f32[1,2048]{1,0:T(1,128)S(1)}, u32[]{:S(2)}, u32[]{:S(2)}) %collective-permute-start.6) | collective-permute-done | bytes 8224 | tf_op jit(solution)/shard_map/ppermute | solution.py:18
  232.6 3.9 collective-permute-start.7
  240.5 7.6 %collective-permute-done.8 = f32[1,2048]{1,0:T(1,128)S(1)} collective-permute-done((f32[1,2048]{1,0:T(1,128)S(1)}, f32[1,2048]{1,0:T(1,128)S(1)}, u32[]{:S(2)}, u32[]{:S(2)}) %collective-permute-start.8) | collective-permute-done | bytes 8224 | tf_op jit(solution)/shard_map/ppermute | solution.py:18
  258.8 18.9 %all_to_all.81 = f32[64,1,2048]{2,1,0:T(1,128)S(1)} all-to-all(f32[64,1,2048]{2,1,0:T(1,128)S(1)} %reshape.650), channel_id=1, replica_groups=mesh['grp'=4,'tile'=64] {'tile'}, dimensions={0} | all-to-all | bytes 1048576 | tf_op jit(solution)/shard_map/all_to_all | solution.py:75
  296.5 19.3 %all_to_all.82 = f32[64,1,2048]{2,1,0:T(1,128)S(1)} all-to-all(f32[64,1,2048]{2,1,0:T(1,128)S(1)} %reshape.652), channel_id=1, replica_groups=mesh['grp'=4,'tile'=64] {'tile'}, dimensions={0} | all-to-all | bytes 1048576 | tf_op jit(solution)/shard_map/all_to_all | solution.py:86
  324.8 38.2 %all-reduce.22.cloned.1.call-done = f32[32,2048]{1,0:T(8,128)} async-done(((f32[32,2048]{1,0:T(8,128)}), f32[32,2048]{1,0:T(8,128)}) %all-reduce.22.cloned.1.call-update) | async-done | bytes 262160 | tf_op jit(solution)/shard_map/psum | solution.py:144
  364.1 8.2 %collective-permute-start.9 = (f32[1,2048]{1,0:T(1,128)S(1)}, f32[1,2048]{1,0:T(1,128)S(1)}, u32[]{:S(2)}, u32[]{:S(2)}) collective-permute-start(f32[1,2048]{1,0:T(1,128)S(1)} %slice.285), channel_id=1, source_target_pairs={{1,0},{2,1},{3,2},{4,3},{5,4},{6,5},{7,6},{8,7},{9,8},{10,9},{11,1... | collective-permute-start | bytes 24584 | tf_op jit(solution)/shard_map/ppermute | solution.py:18
  376.8 8.1 %collective-permute-done.10 = f32[1,2048]{1,0:T(1,128)S(1)} collective-permute-done((f32[1,2048]{1,0:T(1,128)S(1)}, f32[1,2048]{1,0:T(1,128)S(1)}, u32[]{:S(2)}, u32[]{:S(2)}) %collective-permute-start.10) | collective-permute-done | bytes 8224 | tf_op jit(solution)/shard_map/ppermute | solution.py:18
  392.8 7.8 %collective-permute-done.12 = f32[1,2048]{1,0:T(1,128)S(1)} collective-permute-done((f32[1,2048]{1,0:T(1,128)S(1)}, f32[1,2048]{1,0:T(1,128)S(1)}, u32[]{:S(2)}, u32[]{:S(2)}) %collective-permute-start.12) | collective-permute-done | bytes 8224 | tf_op jit(solution)/shard_map/ppermute | solution.py:18
  408.6 7.8 %collective-permute-done.14 = f32[1,2048]{1,0:T(1,128)S(1)} collective-permute-done((f32[1,2048]{1,0:T(1,128)S(1)}, f32[1,2048]{1,0:T(1,128)S(1)}, u32[]{:S(2)}, u32[]{:S(2)}) %collective-permute-start.14) | collective-permute-done | bytes 8224 | tf_op jit(solution)/shard_map/ppermute | solution.py:18
  416.6 3.9 collective-permute-start.15
  424.3 7.8 %collective-permute-done.16 = f32[1,2048]{1,0:T(1,128)S(1)} collective-permute-done((f32[1,2048]{1,0:T(1,128)S(1)}, f32[1,2048]{1,0:T(1,128)S(1)}, u32[]{:S(2)}, u32[]{:S(2)}) %collective-permute-start.16) | collective-permute-done | bytes 8224 | tf_op jit(solution)/shard_map/ppermute | solution.py:18
  (271 shorter events, 145.1 us)
Async XLA Ops:
  15.9 32.0 %all-to-all-start.1 = ((f32[64,1,2048]{2,1,0:T(1,128)}), f32[64,1,2048]{2,1,0:T(1,128)S(1)}, u32[]{:S(2)}, u32[]{:S(2)}) async-start(f32[64,1,2048]{2,1,0:T(1,128)} %reshape.646), calls=%async_computation.1 | async-start | bytes 1048576 | tf_op jit(solution)/shard_map/all_to_all | solution.py:75
  62.8 23.1 %all-to-all-start = ((f32[64,1,2048]{2,1,0:T(1,128)}), f32[64,1,2048]{2,1,0:T(1,128)S(1)}, u32[]{:S(2)}, u32[]{:S(2)}) async-start(f32[64,1,2048]{2,1,0:T(1,128)} %reshape.644), calls=%async_computation | async-start | bytes 1048576 | tf_op jit(solution)/shard_map/all_to_all | solution.py:75
  67.7 111.3 %all-reduce.20.cloned.1.call-start = ((), (), s32[]{:S(2)}) async-start(), calls=%async_computation.5 | async-start | bytes 524288 | tf_op jit(solution)/shard_map/psum | solution.py:144
  138.6 224.5 %all-reduce.22.cloned.1.call-start = ((), (), s32[]{:S(2)}) async-start(), calls=%async_computation.6 | async-start | bytes 524288 | tf_op jit(solution)/shard_map/psum | solution.py:144
  138.6 9.8 %collective-permute-start = (f32[1,2048]{1,0:T(1,128)S(1)}, f32[1,2048]{1,0:T(1,128)S(1)}, u32[]{:S(2)}, u32[]{:S(2)}) collective-permute-start(f32[1,2048]{1,0:T(1,128)S(1)} %broadcast.351), channel_id=1, source_target_pairs={{0,1},{1,2},{2,3},{3,4},{4,5},{5,6},{6,7},{7,8},{8,9},{9,10},{10,1... | collective-permute-start | bytes 24584 | tf_op jit(solution)/shard_map/ppermute | solution.py:18
  179.0 21.9 %copy-start.1 = (f32[32,2048]{1,0:T(8,128)S(1)}, f32[32,2048]{1,0:T(8,128)}, u32[]{:S(2)}) copy-start(f32[32,2048]{1,0:T(8,128)} %all-reduce.20.cloned.1.call-done) | copy-start | bytes 786436
  180.1 9.6 %collective-permute-start.1 = (f32[1,2048]{1,0:T(1,128)S(1)}, f32[1,2048]{1,0:T(1,128)S(1)}, u32[]{:S(2)}, u32[]{:S(2)}) collective-permute-start(f32[1,2048]{1,0:T(1,128)S(1)} %slice.257), channel_id=1, source_target_pairs={{1,0},{2,1},{3,2},{4,3},{5,4},{6,5},{7,6},{8,7},{9,8},{10,9},{11,1... | collective-permute-start | bytes 24584 | tf_op jit(solution)/shard_map/ppermute | solution.py:18
  190.8 10.0 %collective-permute-start.2 = (f32[1,2048]{1,0:T(1,128)S(1)}, f32[1,2048]{1,0:T(1,128)S(1)}, u32[]{:S(2)}, u32[]{:S(2)}) collective-permute-start(f32[1,2048]{1,0:T(1,128)S(1)} %slice.259), channel_id=1, source_target_pairs={{0,1},{1,2},{2,3},{3,4},{4,5},{5,6},{6,7},{7,8},{8,9},{9,10},{10,1... | collective-permute-start | bytes 24584 | tf_op jit(solution)/shard_map/ppermute | solution.py:18
  201.0 5.5 %collective-permute-start.3 = (f32[1,2048]{1,0:T(1,128)S(1)}, f32[1,2048]{1,0:T(1,128)S(1)}, u32[]{:S(2)}, u32[]{:S(2)}) collective-permute-start(f32[1,2048]{1,0:T(1,128)S(1)} %slice.263), channel_id=1, source_target_pairs={{1,0},{2,1},{3,2},{4,3},{5,4},{6,5},{7,6},{8,7},{9,8},{10,9},{11,1... | collective-permute-start | bytes 24584 | tf_op jit(solution)/shard_map/ppermute | solution.py:18
  206.9 9.8 %collective-permute-start.4 = (f32[1,2048]{1,0:T(1,128)S(1)}, f32[1,2048]{1,0:T(1,128)S(1)}, u32[]{:S(2)}, u32[]{:S(2)}) collective-permute-start(f32[1,2048]{1,0:T(1,128)S(1)} %slice.265), channel_id=1, source_target_pairs={{0,1},{1,2},{2,3},{3,4},{4,5},{5,6},{6,7},{7,8},{8,9},{9,10},{10,1... | collective-permute-start | bytes 24584 | tf_op jit(solution)/shard_map/ppermute | solution.py:18
  216.8 5.5 %collective-permute-start.5 = (f32[1,2048]{1,0:T(1,128)S(1)}, f32[1,2048]{1,0:T(1,128)S(1)}, u32[]{:S(2)}, u32[]{:S(2)}) collective-permute-start(f32[1,2048]{1,0:T(1,128)S(1)} %slice.269), channel_id=1, source_target_pairs={{1,0},{2,1},{3,2},{4,3},{5,4},{6,5},{7,6},{8,7},{9,8},{10,9},{11,1... | collective-permute-start | bytes 24584 | tf_op jit(solution)/shard_map/ppermute | solution.py:18
  222.6 9.8 %collective-permute-start.6 = (f32[1,2048]{1,0:T(1,128)S(1)}, f32[1,2048]{1,0:T(1,128)S(1)}, u32[]{:S(2)}, u32[]{:S(2)}) collective-permute-start(f32[1,2048]{1,0:T(1,128)S(1)} %slice.271), channel_id=1, source_target_pairs={{0,1},{1,2},{2,3},{3,4},{4,5},{5,6},{6,7},{7,8},{8,9},{9,10},{10,1... | collective-permute-start | bytes 24584 | tf_op jit(solution)/shard_map/ppermute | solution.py:18
  232.4 15.8 %copy-start.3 = (f32[32,2048]{1,0:T(8,128)S(1)}, f32[32,2048]{1,0:T(8,128)}, u32[]{:S(2)}) copy-start(f32[32,2048]{1,0:T(8,128)} %copy.460) | copy-start | bytes 786436
  232.6 5.5 %collective-permute-start.7 = (f32[1,2048]{1,0:T(1,128)S(1)}, f32[1,2048]{1,0:T(1,128)S(1)}, u32[]{:S(2)}, u32[]{:S(2)}) collective-permute-start(f32[1,2048]{1,0:T(1,128)S(1)} %slice.275), channel_id=1, source_target_pairs={{1,0},{2,1},{3,2},{4,3},{5,4},{6,5},{7,6},{8,7},{9,8},{10,9},{11,1... | collective-permute-start | bytes 24584 | tf_op jit(solution)/shard_map/ppermute | solution.py:18
  238.4 9.8 %collective-permute-start.8 = (f32[1,2048]{1,0:T(1,128)S(1)}, f32[1,2048]{1,0:T(1,128)S(1)}, u32[]{:S(2)}, u32[]{:S(2)}) collective-permute-start(f32[1,2048]{1,0:T(1,128)S(1)} %slice.277), channel_id=1, source_target_pairs={{0,1},{1,2},{2,3},{3,4},{4,5},{5,6},{6,7},{7,8},{8,9},{9,10},{10,1... | collective-permute-start | bytes 24584 | tf_op jit(solution)/shard_map/ppermute | solution.py:18
  363.0 21.9 %copy-start = (f32[32,2048]{1,0:T(8,128)S(1)}, f32[32,2048]{1,0:T(8,128)}, u32[]{:S(2)}) copy-start(f32[32,2048]{1,0:T(8,128)} %all-reduce.22.cloned.1.call-done) | copy-start | bytes 786436
  364.1 9.6 %collective-permute-start.9 = (f32[1,2048]{1,0:T(1,128)S(1)}, f32[1,2048]{1,0:T(1,128)S(1)}, u32[]{:S(2)}, u32[]{:S(2)}) collective-permute-start(f32[1,2048]{1,0:T(1,128)S(1)} %slice.285), channel_id=1, source_target_pairs={{1,0},{2,1},{3,2},{4,3},{5,4},{6,5},{7,6},{8,7},{9,8},{10,9},{11,1... | collective-permute-start | bytes 24584 | tf_op jit(solution)/shard_map/ppermute | solution.py:18
  374.9 10.0 %collective-permute-start.10 = (f32[1,2048]{1,0:T(1,128)S(1)}, f32[1,2048]{1,0:T(1,128)S(1)}, u32[]{:S(2)}, u32[]{:S(2)}) collective-permute-start(f32[1,2048]{1,0:T(1,128)S(1)} %slice.287), channel_id=1, source_target_pairs={{0,1},{1,2},{2,3},{3,4},{4,5},{5,6},{6,7},{7,8},{8,9},{9,10},{10,1... | collective-permute-start | bytes 24584 | tf_op jit(solution)/shard_map/ppermute | solution.py:18
  385.1 5.5 %collective-permute-start.11 = (f32[1,2048]{1,0:T(1,128)S(1)}, f32[1,2048]{1,0:T(1,128)S(1)}, u32[]{:S(2)}, u32[]{:S(2)}) collective-permute-start(f32[1,2048]{1,0:T(1,128)S(1)} %slice.291), channel_id=1, source_target_pairs={{1,0},{2,1},{3,2},{4,3},{5,4},{6,5},{7,6},{8,7},{9,8},{10,9},{11,1... | collective-permute-start | bytes 24584 | tf_op jit(solution)/shard_map/ppermute | solution.py:18
  390.9 9.8 %collective-permute-start.12 = (f32[1,2048]{1,0:T(1,128)S(1)}, f32[1,2048]{1,0:T(1,128)S(1)}, u32[]{:S(2)}, u32[]{:S(2)}) collective-permute-start(f32[1,2048]{1,0:T(1,128)S(1)} %slice.293), channel_id=1, source_target_pairs={{0,1},{1,2},{2,3},{3,4},{4,5},{5,6},{6,7},{7,8},{8,9},{9,10},{10,1... | collective-permute-start | bytes 24584 | tf_op jit(solution)/shard_map/ppermute | solution.py:18
  400.8 5.5 %collective-permute-start.13 = (f32[1,2048]{1,0:T(1,128)S(1)}, f32[1,2048]{1,0:T(1,128)S(1)}, u32[]{:S(2)}, u32[]{:S(2)}) collective-permute-start(f32[1,2048]{1,0:T(1,128)S(1)} %slice.297), channel_id=1, source_target_pairs={{1,0},{2,1},{3,2},{4,3},{5,4},{6,5},{7,6},{8,7},{9,8},{10,9},{11,1... | collective-permute-start | bytes 24584 | tf_op jit(solution)/shard_map/ppermute | solution.py:18
  406.6 9.8 %collective-permute-start.14 = (f32[1,2048]{1,0:T(1,128)S(1)}, f32[1,2048]{1,0:T(1,128)S(1)}, u32[]{:S(2)}, u32[]{:S(2)}) collective-permute-start(f32[1,2048]{1,0:T(1,128)S(1)} %slice.299), channel_id=1, source_target_pairs={{0,1},{1,2},{2,3},{3,4},{4,5},{5,6},{6,7},{7,8},{8,9},{9,10},{10,1... | collective-permute-start | bytes 24584 | tf_op jit(solution)/shard_map/ppermute | solution.py:18
  416.6 5.5 %collective-permute-start.15 = (f32[1,2048]{1,0:T(1,128)S(1)}, f32[1,2048]{1,0:T(1,128)S(1)}, u32[]{:S(2)}, u32[]{:S(2)}) collective-permute-start(f32[1,2048]{1,0:T(1,128)S(1)} %slice.303), channel_id=1, source_target_pairs={{1,0},{2,1},{3,2},{4,3},{5,4},{6,5},{7,6},{8,7},{9,8},{10,9},{11,1... | collective-permute-start | bytes 24584 | tf_op jit(solution)/shard_map/ppermute | solution.py:18
  422.4 9.8 %collective-permute-start.16 = (f32[1,2048]{1,0:T(1,128)S(1)}, f32[1,2048]{1,0:T(1,128)S(1)}, u32[]{:S(2)}, u32[]{:S(2)}) collective-permute-start(f32[1,2048]{1,0:T(1,128)S(1)} %slice.305), channel_id=1, source_target_pairs={{0,1},{1,2},{2,3},{3,4},{4,5},{5,6},{6,7},{7,8},{8,9},{9,10},{10,1... | collective-permute-start | bytes 24584 | tf_op jit(solution)/shard_map/ppermute | solution.py:18
  (6 other events, 35.0 us)
Sparse Core Ops, SparseCore 0:
  138.7 40.2 all-reduce.19
  324.9 38.0 all-reduce.21
where the time goes:
time: 447 us; the launch traced here: 440 us
  waiting for transfers between devices  180 us (40%)
  starting transfers between devices  76.9 us (17%)
  blocking collectives  60.6 us (14%)
  local copies, waits for them, and re-layouts  50.5 us (11%)
  matrix products  37.6 us (8%)
  other arithmetic  19.4 us (4%)
  between operations  15.3 us (3%)
    ppermute x17, waiting for transfers between devices, from_behind(): lax.ppermute(value, axis, [(source, source + steps) for source in range(l...  81 us
    psum x2, waiting for transfers between devices, body(): average = lax.psum(partial_sum, 'grp') / total_frames  68.9 us
    ppermute x17, starting transfers between devices, from_behind(): lax.ppermute(value, axis, [(source, source + steps) for source in range(l...  58.4 us
    all_to_all x2, blocking collectives, to_image(): lax.all_to_all(packed, 'tile', split_axis=0, concat_axis=1, tiled=True)  41.8 us
    all_to_all x2, waiting for transfers between devices, to_spectrum(): lax.all_to_all(packed, 'tile', split_axis=0, concat_axis=1, tiled=True)  29.7 us
    all_to_all x1, blocking collectives, to_spectrum(): lax.all_to_all(packed, 'tile', split_axis=0, concat_axis=1, tiled=True)  18.9 us
    all_to_all x2, starting transfers between devices, to_spectrum(): lax.all_to_all(packed, 'tile', split_axis=0, concat_axis=1, tiled=True)  18.3 us
    unnamed x34, local copies, waits for them, and re-layouts  12 us
  transfers between devices with their start and end apart: 21, of which 21 were waited for; matrix products, arithmetic and copies ran while one was open for 2% of the time, Pallas kernels for 0%

commit v1 on v0

--- a/solution.py
+++ b/solution.py
@@ -141,7 +141,8 @@
             (weighted_imag + penalty * shifted_imag) * gain,
         )
         partial_sum = jnp.sum(estimates + duals, axis=0)
-        average = lax.psum(partial_sum, "grp") / total_frames
+        fit_islands = lambda u_in: jax.lax.all_gather(u_in, axis_name="grp").sum(axis=0)
+        average = fit_islands(partial_sum) / total_frames
         consensus = denoise(average)
         duals = duals + estimates - consensus[None]
     return consensus

time: 447 us -> 400 us (0.89)
  waiting for transfers between devices: 180 us -> 134 us
    psum x2 -> x0, waiting for transfers between devices: 68.9 us -> none  [body(): average = lax.psum(partial_sum, 'grp') / total_frames]
    all_gather x0 -> x2, waiting for transfers between devices: none -> 30.8 us  [body(): jax.lax.all_gather(u_in, axis_name='grp').sum(axis=0)]
    ppermute x17, waiting for transfers between devices: 81 us -> 73.8 us  [from_behind(): lax.ppermute(value, axis, [(source, source + steps) for source in range(l...]
    unnamed x34 -> x28, local copies, waits for them, and re-layouts: 12 us -> 12 us
  transfers between devices with their start and end apart: 21 -> 21, of which waited for: 21 -> 20; matrix products, arithmetic and copies ran while one was open for 2% -> 2% of each run, Pallas kernels for 0% -> 0%
where the time goes in v1:
time: 400 us; the launch traced here: 394 us
  waiting for transfers between devices  134 us (34%)
  starting transfers between devices  77 us (19%)
  blocking collectives  60.6 us (15%)
  local copies, waits for them, and re-layouts  50.8 us (13%)
  matrix products  37.6 us (9%)
  other arithmetic  17.8 us (4%)
  between operations  15.4 us (4%)
    ppermute x17, waiting for transfers between devices, from_behind(): lax.ppermute(value, axis, [(source, source + steps) for source in range(l...  73.8 us
    ppermute x17, starting transfers between devices, from_behind(): lax.ppermute(value, axis, [(source, source + steps) for source in range(l...  58.4 us
    all_to_all x2, blocking collectives, to_image(): lax.all_to_all(packed, 'tile', split_axis=0, concat_axis=1, tiled=True)  41.7 us
    all_gather x2, waiting for transfers between devices, body(): jax.lax.all_gather(u_in, axis_name='grp').sum(axis=0)  30.8 us
    all_to_all x2, waiting for transfers between devices, to_spectrum(): lax.all_to_all(packed, 'tile', split_axis=0, concat_axis=1, tiled=True)  29.7 us
    all_to_all x1, blocking collectives, to_spectrum(): lax.all_to_all(packed, 'tile', split_axis=0, concat_axis=1, tiled=True)  18.9 us
    all_to_all x2, starting transfers between devices, to_spectrum(): lax.all_to_all(packed, 'tile', split_axis=0, concat_axis=1, tiled=True)  18.3 us
    unnamed x28, local copies, waits for them, and re-layouts  12 us
  transfers between devices with their start and end apart: 21, of which 20 were waited for; matrix products, arithmetic and copies ran while one was open for 2% of the time, Pallas kernels for 0%

profile of v1, /device:TPU:8, one launch (start us, length us, event | category | flops | bytes accessed | tf_op | source)
XLA Modules:
  0.0 393.5 jit_solution(18265783277875700476)
XLA Ops:
  16.0 13.3 %all-to-all-start.1 = ((f32[64,1,2048]{2,1,0:T(1,128)}), f32[64,1,2048]{2,1,0:T(1,128)S(1)}, u32[]{:S(2)}, u32[]{:S(2)}) async-start(f32[64,1,2048]{2,1,0:T(1,128)} %reshape.661), calls=%async_computation.1 | async-start | bytes 1048576 | tf_op jit(solution)/shard_map/all_to_all | solution.py:75
  30.2 17.7 %all-to-all-done.1 = f32[64,1,2048]{2,1,0:T(1,128)S(1)} async-done(((f32[64,1,2048]{2,1,0:T(1,128)}), f32[64,1,2048]{2,1,0:T(1,128)S(1)}, u32[]{:S(2)}, u32[]{:S(2)}) %all-to-all-start.1) | async-done | bytes 524320 | tf_op jit(solution)/shard_map/all_to_all | solution.py:75
  62.7 5.0 %all-to-all-start = ((f32[64,1,2048]{2,1,0:T(1,128)}), f32[64,1,2048]{2,1,0:T(1,128)S(1)}, u32[]{:S(2)}, u32[]{:S(2)}) async-start(f32[64,1,2048]{2,1,0:T(1,128)} %reshape.659), calls=%async_computation | async-start | bytes 1048576 | tf_op jit(solution)/shard_map/all_to_all | solution.py:75
  73.8 12.0 %all-to-all-done = f32[64,1,2048]{2,1,0:T(1,128)S(1)} async-done(((f32[64,1,2048]{2,1,0:T(1,128)}), f32[64,1,2048]{2,1,0:T(1,128)S(1)}, u32[]{:S(2)}, u32[]{:S(2)}) %all-to-all-start) | async-done | bytes 524320 | tf_op jit(solution)/shard_map/all_to_all | solution.py:75
  107.2 22.4 %all_to_all.80 = f32[64,1,2048]{2,1,0:T(1,128)S(1)} all-to-all(f32[64,1,2048]{2,1,0:T(1,128)S(1)} %reshape.663), channel_id=1, replica_groups=mesh['grp'=4,'tile'=64] {'tile'}, dimensions={0} | all-to-all | bytes 1048576 | tf_op jit(solution)/shard_map/all_to_all | solution.py:86
  141.3 15.1 %all-gather.4.cloned.1.call-done = f32[4,32,2048]{2,1,0:T(8,128)} async-done(((f32[1,32,2048]{2,1,0:T(8,128)}), f32[4,32,2048]{2,1,0:T(8,128)}) %all-gather.4.cloned.1.call-update) | async-done | bytes 1048592 | tf_op jit(solution)/shard_map/all_gather | solution.py:144
  157.8 8.2 %collective-permute-start.1 = (f32[1,2048]{1,0:T(1,128)S(1)}, f32[1,2048]{1,0:T(1,128)S(1)}, u32[]{:S(2)}, u32[]{:S(2)}) collective-permute-start(f32[1,2048]{1,0:T(1,128)S(1)} %slice.257), channel_id=1, source_target_pairs={{1,0},{2,1},{3,2},{4,3},{5,4},{6,5},{7,6},{8,7},{9,8},{10,9},{11,1... | collective-permute-start | bytes 24584 | tf_op jit(solution)/shard_map/ppermute | solution.py:18
  169.5 8.1 %collective-permute-done.2 = f32[1,2048]{1,0:T(1,128)S(1)} collective-permute-done((f32[1,2048]{1,0:T(1,128)S(1)}, f32[1,2048]{1,0:T(1,128)S(1)}, u32[]{:S(2)}, u32[]{:S(2)}) %collective-permute-start.2) | collective-permute-done | bytes 8224 | tf_op jit(solution)/shard_map/ppermute | solution.py:18
  177.8 3.9 collective-permute-start.3
  185.6 7.8 %collective-permute-done.4 = f32[1,2048]{1,0:T(1,128)S(1)} collective-permute-done((f32[1,2048]{1,0:T(1,128)S(1)}, f32[1,2048]{1,0:T(1,128)S(1)}, u32[]{:S(2)}, u32[]{:S(2)}) %collective-permute-start.4) | collective-permute-done | bytes 8224 | tf_op jit(solution)/shard_map/ppermute | solution.py:18
  193.6 3.9 collective-permute-start.5
  201.3 7.8 %collective-permute-done.6 = f32[1,2048]{1,0:T(1,128)S(1)} collective-permute-done((f32[1,2048]{1,0:T(1,128)S(1)}, f32[1,2048]{1,0:T(1,128)S(1)}, u32[]{:S(2)}, u32[]{:S(2)}) %collective-permute-start.6) | collective-permute-done | bytes 8224 | tf_op jit(solution)/shard_map/ppermute | solution.py:18
  209.3 3.9 collective-permute-start.7
  217.6 7.3 %collective-permute-done.8 = f32[1,2048]{1,0:T(1,128)S(1)} collective-permute-done((f32[1,2048]{1,0:T(1,128)S(1)}, f32[1,2048]{1,0:T(1,128)S(1)}, u32[]{:S(2)}, u32[]{:S(2)}) %collective-permute-start.8) | collective-permute-done | bytes 8224 | tf_op jit(solution)/shard_map/ppermute | solution.py:18
  235.6 18.9 %all_to_all.81 = f32[64,1,2048]{2,1,0:T(1,128)S(1)} all-to-all(f32[64,1,2048]{2,1,0:T(1,128)S(1)} %reshape.665), channel_id=1, replica_groups=mesh['grp'=4,'tile'=64] {'tile'}, dimensions={0} | all-to-all | bytes 1048576 | tf_op jit(solution)/shard_map/all_to_all | solution.py:75
  273.2 19.3 %all_to_all.82 = f32[64,1,2048]{2,1,0:T(1,128)S(1)} all-to-all(f32[64,1,2048]{2,1,0:T(1,128)S(1)} %reshape.667), channel_id=1, replica_groups=mesh['grp'=4,'tile'=64] {'tile'}, dimensions={0} | all-to-all | bytes 1048576 | tf_op jit(solution)/shard_map/all_to_all | solution.py:86
  301.4 15.8 %all-gather.6.cloned.1.call-done = f32[128,2048]{1,0:T(8,128)} async-done(((f32[32,2048]{1,0:T(8,128)}), f32[128,2048]{1,0:T(8,128)}) %all-gather.6.cloned.1.call-update) | async-done | bytes 1048592 | tf_op jit(solution)/shard_map/all_gather | solution.py:144
  318.5 8.2 %collective-permute-start.9 = (f32[1,2048]{1,0:T(1,128)S(1)}, f32[1,2048]{1,0:T(1,128)S(1)}, u32[]{:S(2)}, u32[]{:S(2)}) collective-permute-start(f32[1,2048]{1,0:T(1,128)S(1)} %slice.285), channel_id=1, source_target_pairs={{1,0},{2,1},{3,2},{4,3},{5,4},{6,5},{7,6},{8,7},{9,8},{10,9},{11,1... | collective-permute-start | bytes 24584 | tf_op jit(solution)/shard_map/ppermute | solution.py:18
  330.3 8.1 %collective-permute-done.10 = f32[1,2048]{1,0:T(1,128)S(1)} collective-permute-done((f32[1,2048]{1,0:T(1,128)S(1)}, f32[1,2048]{1,0:T(1,128)S(1)}, u32[]{:S(2)}, u32[]{:S(2)}) %collective-permute-start.10) | collective-permute-done | bytes 8224 | tf_op jit(solution)/shard_map/ppermute | solution.py:18
  338.6 3.9 collective-permute-start.11
  346.3 7.8 %collective-permute-done.12 = f32[1,2048]{1,0:T(1,128)S(1)} collective-permute-done((f32[1,2048]{1,0:T(1,128)S(1)}, f32[1,2048]{1,0:T(1,128)S(1)}, u32[]{:S(2)}, u32[]{:S(2)}) %collective-permute-start.12) | collective-permute-done | bytes 8224 | tf_op jit(solution)/shard_map/ppermute | solution.py:18
  354.3 3.9 collective-permute-start.13
  362.1 7.8 %collective-permute-done.14 = f32[1,2048]{1,0:T(1,128)S(1)} collective-permute-done((f32[1,2048]{1,0:T(1,128)S(1)}, f32[1,2048]{1,0:T(1,128)S(1)}, u32[]{:S(2)}, u32[]{:S(2)}) %collective-permute-start.14) | collective-permute-done | bytes 8224 | tf_op jit(solution)/shard_map/ppermute | solution.py:18
  377.8 7.8 %collective-permute-done.16 = f32[1,2048]{1,0:T(1,128)S(1)} collective-permute-done((f32[1,2048]{1,0:T(1,128)S(1)}, f32[1,2048]{1,0:T(1,128)S(1)}, u32[]{:S(2)}, u32[]{:S(2)}) %collective-permute-start.16) | collective-permute-done | bytes 8224 | tf_op jit(solution)/shard_map/ppermute | solution.py:18
  (268 shorter events, 139.9 us)
Async XLA Ops:
  14.5 14.8 %copy-start.5 = (f32[1,32,2048]{2,1,0:T(8,128)S(1)}, f32[1,32,2048]{2,1,0:T(8,128)}, u32[]{:S(2)}) copy-start(f32[1,32,2048]{2,1,0:T(8,128)} %param.3) | copy-start | bytes 786436
  16.0 32.0 %all-to-all-start.1 = ((f32[64,1,2048]{2,1,0:T(1,128)}), f32[64,1,2048]{2,1,0:T(1,128)S(1)}, u32[]{:S(2)}, u32[]{:S(2)}) async-start(f32[64,1,2048]{2,1,0:T(1,128)} %reshape.661), calls=%async_computation.1 | async-start | bytes 1048576 | tf_op jit(solution)/shard_map/all_to_all | solution.py:75
  61.3 6.7 %copy-start.4 = (f32[1,2,32,2048]{3,2,1,0:T(8,128)S(1)}, f32[1,2,32,2048]{3,2,1,0:T(8,128)}, u32[]{:S(2)}) copy-start(f32[1,2,32,2048]{3,2,1,0:T(8,128)} %param.4) | copy-start | bytes 1572868
  61.3 8.3 %copy-start = (f32[32,16,128]{2,1,0:T(8,128)S(1)}, f32[32,16,128]{2,1,0:T(8,128)}, u32[]{:S(2)}) copy-start(f32[32,16,128]{2,1,0:T(8,128)} %get-tuple-element.48) | copy-start | bytes 786436
  62.7 23.1 %all-to-all-start = ((f32[64,1,2048]{2,1,0:T(1,128)}), f32[64,1,2048]{2,1,0:T(1,128)S(1)}, u32[]{:S(2)}, u32[]{:S(2)}) async-start(f32[64,1,2048]{2,1,0:T(1,128)} %reshape.659), calls=%async_computation | async-start | bytes 1048576 | tf_op jit(solution)/shard_map/all_to_all | solution.py:75
  67.7 88.7 %all-gather.4.cloned.1.call-start = ((), (), s32[]{:S(2)}) async-start(), calls=%async_computation.5 | async-start | bytes 1310720 | tf_op jit(solution)/shard_map/all_gather | solution.py:144
  138.4 178.7 %all-gather.6.cloned.1.call-start = ((), (), s32[]{:S(2)}) async-start(), calls=%async_computation.6 | async-start | bytes 1310720 | tf_op jit(solution)/shard_map/all_gather | solution.py:144
  138.5 19.2 %collective-permute-start = (f32[1,2048]{1,0:T(1,128)S(1)}, f32[1,2048]{1,0:T(1,128)S(1)}, u32[]{:S(2)}, u32[]{:S(2)}) collective-permute-start(f32[1,2048]{1,0:T(1,128)S(1)} %broadcast.363), channel_id=1, source_target_pairs={{0,1},{1,2},{2,3},{3,4},{4,5},{5,6},{6,7},{7,8},{8,9},{9,10},{10,1... | collective-permute-start | bytes 24584 | tf_op jit(solution)/shard_map/ppermute | solution.py:18
  157.8 9.6 %collective-permute-start.1 = (f32[1,2048]{1,0:T(1,128)S(1)}, f32[1,2048]{1,0:T(1,128)S(1)}, u32[]{:S(2)}, u32[]{:S(2)}) collective-permute-start(f32[1,2048]{1,0:T(1,128)S(1)} %slice.257), channel_id=1, source_target_pairs={{1,0},{2,1},{3,2},{4,3},{5,4},{6,5},{7,6},{8,7},{9,8},{10,9},{11,1... | collective-permute-start | bytes 24584 | tf_op jit(solution)/shard_map/ppermute | solution.py:18
  167.6 10.0 %collective-permute-start.2 = (f32[1,2048]{1,0:T(1,128)S(1)}, f32[1,2048]{1,0:T(1,128)S(1)}, u32[]{:S(2)}, u32[]{:S(2)}) collective-permute-start(f32[1,2048]{1,0:T(1,128)S(1)} %slice.259), channel_id=1, source_target_pairs={{0,1},{1,2},{2,3},{3,4},{4,5},{5,6},{6,7},{7,8},{8,9},{9,10},{10,1... | collective-permute-start | bytes 24584 | tf_op jit(solution)/shard_map/ppermute | solution.py:18
  177.8 5.5 %collective-permute-start.3 = (f32[1,2048]{1,0:T(1,128)S(1)}, f32[1,2048]{1,0:T(1,128)S(1)}, u32[]{:S(2)}, u32[]{:S(2)}) collective-permute-start(f32[1,2048]{1,0:T(1,128)S(1)} %slice.263), channel_id=1, source_target_pairs={{1,0},{2,1},{3,2},{4,3},{5,4},{6,5},{7,6},{8,7},{9,8},{10,9},{11,1... | collective-permute-start | bytes 24584 | tf_op jit(solution)/shard_map/ppermute | solution.py:18
  183.6 9.8 %collective-permute-start.4 = (f32[1,2048]{1,0:T(1,128)S(1)}, f32[1,2048]{1,0:T(1,128)S(1)}, u32[]{:S(2)}, u32[]{:S(2)}) collective-permute-start(f32[1,2048]{1,0:T(1,128)S(1)} %slice.265), channel_id=1, source_target_pairs={{0,1},{1,2},{2,3},{3,4},{4,5},{5,6},{6,7},{7,8},{8,9},{9,10},{10,1... | collective-permute-start | bytes 24584 | tf_op jit(solution)/shard_map/ppermute | solution.py:18
  193.6 5.5 %collective-permute-start.5 = (f32[1,2048]{1,0:T(1,128)S(1)}, f32[1,2048]{1,0:T(1,128)S(1)}, u32[]{:S(2)}, u32[]{:S(2)}) collective-permute-start(f32[1,2048]{1,0:T(1,128)S(1)} %slice.269), channel_id=1, source_target_pairs={{1,0},{2,1},{3,2},{4,3},{5,4},{6,5},{7,6},{8,7},{9,8},{10,9},{11,1... | collective-permute-start | bytes 24584 | tf_op jit(solution)/shard_map/ppermute | solution.py:18
  199.4 9.8 %collective-permute-start.6 = (f32[1,2048]{1,0:T(1,128)S(1)}, f32[1,2048]{1,0:T(1,128)S(1)}, u32[]{:S(2)}, u32[]{:S(2)}) collective-permute-start(f32[1,2048]{1,0:T(1,128)S(1)} %slice.271), channel_id=1, source_target_pairs={{0,1},{1,2},{2,3},{3,4},{4,5},{5,6},{6,7},{7,8},{8,9},{9,10},{10,1... | collective-permute-start | bytes 24584 | tf_op jit(solution)/shard_map/ppermute | solution.py:18
  209.3 5.5 %collective-permute-start.7 = (f32[1,2048]{1,0:T(1,128)S(1)}, f32[1,2048]{1,0:T(1,128)S(1)}, u32[]{:S(2)}, u32[]{:S(2)}) collective-permute-start(f32[1,2048]{1,0:T(1,128)S(1)} %slice.275), channel_id=1, source_target_pairs={{1,0},{2,1},{3,2},{4,3},{5,4},{6,5},{7,6},{8,7},{9,8},{10,9},{11,1... | collective-permute-start | bytes 24584 | tf_op jit(solution)/shard_map/ppermute | solution.py:18
  215.1 9.8 %collective-permute-start.8 = (f32[1,2048]{1,0:T(1,128)S(1)}, f32[1,2048]{1,0:T(1,128)S(1)}, u32[]{:S(2)}, u32[]{:S(2)}) collective-permute-start(f32[1,2048]{1,0:T(1,128)S(1)} %slice.277), channel_id=1, source_target_pairs={{0,1},{1,2},{2,3},{3,4},{4,5},{5,6},{6,7},{7,8},{8,9},{9,10},{10,1... | collective-permute-start | bytes 24584 | tf_op jit(solution)/shard_map/ppermute | solution.py:18
  318.5 9.6 %collective-permute-start.9 = (f32[1,2048]{1,0:T(1,128)S(1)}, f32[1,2048]{1,0:T(1,128)S(1)}, u32[]{:S(2)}, u32[]{:S(2)}) collective-permute-start(f32[1,2048]{1,0:T(1,128)S(1)} %slice.285), channel_id=1, source_target_pairs={{1,0},{2,1},{3,2},{4,3},{5,4},{6,5},{7,6},{8,7},{9,8},{10,9},{11,1... | collective-permute-start | bytes 24584 | tf_op jit(solution)/shard_map/ppermute | solution.py:18
  328.4 10.0 %collective-permute-start.10 = (f32[1,2048]{1,0:T(1,128)S(1)}, f32[1,2048]{1,0:T(1,128)S(1)}, u32[]{:S(2)}, u32[]{:S(2)}) collective-permute-start(f32[1,2048]{1,0:T(1,128)S(1)} %slice.287), channel_id=1, source_target_pairs={{0,1},{1,2},{2,3},{3,4},{4,5},{5,6},{6,7},{7,8},{8,9},{9,10},{10,1... | collective-permute-start | bytes 24584 | tf_op jit(solution)/shard_map/ppermute | solution.py:18
  338.6 5.5 %collective-permute-start.11 = (f32[1,2048]{1,0:T(1,128)S(1)}, f32[1,2048]{1,0:T(1,128)S(1)}, u32[]{:S(2)}, u32[]{:S(2)}) collective-permute-start(f32[1,2048]{1,0:T(1,128)S(1)} %slice.291), channel_id=1, source_target_pairs={{1,0},{2,1},{3,2},{4,3},{5,4},{6,5},{7,6},{8,7},{9,8},{10,9},{11,1... | collective-permute-start | bytes 24584 | tf_op jit(solution)/shard_map/ppermute | solution.py:18
  344.4 9.8 %collective-permute-start.12 = (f32[1,2048]{1,0:T(1,128)S(1)}, f32[1,2048]{1,0:T(1,128)S(1)}, u32[]{:S(2)}, u32[]{:S(2)}) collective-permute-start(f32[1,2048]{1,0:T(1,128)S(1)} %slice.293), channel_id=1, source_target_pairs={{0,1},{1,2},{2,3},{3,4},{4,5},{5,6},{6,7},{7,8},{8,9},{9,10},{10,1... | collective-permute-start | bytes 24584 | tf_op jit(solution)/shard_map/ppermute | solution.py:18
  354.3 5.5 %collective-permute-start.13 = (f32[1,2048]{1,0:T(1,128)S(1)}, f32[1,2048]{1,0:T(1,128)S(1)}, u32[]{:S(2)}, u32[]{:S(2)}) collective-permute-start(f32[1,2048]{1,0:T(1,128)S(1)} %slice.297), channel_id=1, source_target_pairs={{1,0},{2,1},{3,2},{4,3},{5,4},{6,5},{7,6},{8,7},{9,8},{10,9},{11,1... | collective-permute-start | bytes 24584 | tf_op jit(solution)/shard_map/ppermute | solution.py:18
  360.2 9.8 %collective-permute-start.14 = (f32[1,2048]{1,0:T(1,128)S(1)}, f32[1,2048]{1,0:T(1,128)S(1)}, u32[]{:S(2)}, u32[]{:S(2)}) collective-permute-start(f32[1,2048]{1,0:T(1,128)S(1)} %slice.299), channel_id=1, source_target_pairs={{0,1},{1,2},{2,3},{3,4},{4,5},{5,6},{6,7},{7,8},{8,9},{9,10},{10,1... | collective-permute-start | bytes 24584 | tf_op jit(solution)/shard_map/ppermute | solution.py:18
  370.1 5.5 %collective-permute-start.15 = (f32[1,2048]{1,0:T(1,128)S(1)}, f32[1,2048]{1,0:T(1,128)S(1)}, u32[]{:S(2)}, u32[]{:S(2)}) collective-permute-start(f32[1,2048]{1,0:T(1,128)S(1)} %slice.303), channel_id=1, source_target_pairs={{1,0},{2,1},{3,2},{4,3},{5,4},{6,5},{7,6},{8,7},{9,8},{10,9},{11,1... | collective-permute-start | bytes 24584 | tf_op jit(solution)/shard_map/ppermute | solution.py:18
  375.9 9.8 %collective-permute-start.16 = (f32[1,2048]{1,0:T(1,128)S(1)}, f32[1,2048]{1,0:T(1,128)S(1)}, u32[]{:S(2)}, u32[]{:S(2)}) collective-permute-start(f32[1,2048]{1,0:T(1,128)S(1)} %slice.305), channel_id=1, source_target_pairs={{0,1},{1,2},{2,3},{3,4},{4,5},{5,6},{6,7},{7,8},{8,9},{9,10},{10,1... | collective-permute-start | bytes 24584 | tf_op jit(solution)/shard_map/ppermute | solution.py:18
  (3 other events, 5.3 us)
Sparse Core Ops, SparseCore 0:
  138.6 17.8 all-gather.3
  301.5 15.5 all-gather.5
